TPU v7x, 512 devices: a whole 4x8x8 slice. The times are simulated.
512 devices in a mesh: dp: 2 (over core), section: 4 (over x), expert: 64 (over y, z).
Axes of the slice: x: 4, y: 8, z: 8, core: 2. Of those that a mesh axis runs over, the one named last changes fastest.
Arguments:
- grad_out: bfloat16 [16384, 3584], P(('dp', 'expert'), 'section'), may hold values from -6 to 6
- expert_ids: int32 [16384, 8], P(('dp', 'expert')), may hold values from 0 to 63, all different within a row; in each aligned block of 128 rows (0 to 127, 128 to 255, ...) at most 24 rows name the same one
- gate_weights: float32 [16384, 8], P(('dp', 'expert')), may hold values from 0.1 to 1
- act: bfloat16 [16384, 8, 1024], P(('dp', 'expert'), None, 'section'), may hold values from -0.8984375 to 0.8984375
- w_down: bfloat16 [64, 1024, 3584], P('expert', 'section'), may hold values from -0.09375 to 0.09375
Outputs:
- grad_hidden: bfloat16 [16384, 8, 1024], P(('dp', 'expert'), None, 'section')
- grad_gates: float32 [16384, 8], P(('dp', 'expert'))
- grad_w: bfloat16 [64, 1024, 3584], P('expert', 'section', 'dp')
Inputs may be any that keep to these rules, and one draw needn't show every extreme that they name: `expert_ids`: each row names 8 different experts. In each aligned block of 128 rows (the tokens of one device) no expert is named by more than 24 rows, and in every draw some expert is named by exactly 24 rows of some block.
All inputs are finite; a program needn't handle non-finite values.
Results may differ from a plain program's by a relative error of at most 0.0058.
Values may be sent and summed in bfloat16 or wider, within the bound.
No kernel may reach another device: no remote copies, remote signals or barrier semaphores. Data moves between devices by JAX's collectives and lax.ppermute only.
A program may use at most 64 MiB of HBM per device.

v0:
```python
import jax
import jax.numpy as jnp
from jax import lax
from jax.sharding import PartitionSpec as P


def routing(expert_ids, experts, capacity):
    tok_count, top_count = expert_ids.shape
    onehot = expert_ids[:, :, None] == jnp.arange(experts, dtype=jnp.int32)[None, None, :]
    per_token = jnp.any(onehot, axis=1).astype(jnp.bfloat16)
    rows = jnp.arange(tok_count, dtype=jnp.int32)
    lower = (rows[:, None] > rows[None, :]).astype(jnp.bfloat16)
    before = jnp.dot(lower, per_token, preferred_element_type=jnp.float32)
    order_in = jnp.sum(jnp.where(onehot, before[:, None, :], 0.0), axis=2).astype(jnp.int32)
    position = expert_ids * capacity + order_in
    slots = jnp.arange(experts * capacity, dtype=jnp.int32)
    sel_pairs = position.reshape(tok_count * top_count)[None, :] == slots[:, None]
    pairs = jnp.arange(tok_count * top_count, dtype=jnp.int32)
    member = (pairs[:, None] // top_count == rows[None, :]).astype(jnp.bfloat16)
    sel_pairs = sel_pairs.astype(jnp.bfloat16)
    sel_tok = jnp.dot(sel_pairs, member, preferred_element_type=jnp.float32).astype(jnp.bfloat16)
    return (sel_pairs, sel_tok)


def local(grad_out, expert_ids, gate_weights, act, w_down):
    tok_count, top_count = expert_ids.shape
    hidden_slice = act.shape[2]
    d_slice = grad_out.shape[1]
    n_expert = lax.axis_size("expert")
    n_section = lax.axis_size("section")
    experts = w_down.shape[0] * n_expert
    capacity = 3 * tok_count * top_count // (2 * experts)
    pair_count = tok_count * top_count
    slot_count = experts * capacity
    sel_pairs, sel_tok = routing(expert_ids, experts, capacity)
    scaled = (
        (gate_weights[:, :, None] * act.astype(jnp.float32))
        .astype(jnp.bfloat16)
        .reshape(pair_count, hidden_slice)
    )
    send_scaled = jnp.dot(sel_pairs, scaled, preferred_element_type=jnp.float32).astype(
        jnp.bfloat16
    )
    send_grad = jnp.dot(sel_tok, grad_out, preferred_element_type=jnp.float32).astype(jnp.bfloat16)
    send = jnp.concatenate([send_grad, send_scaled], axis=1).reshape(
        experts, capacity, d_slice + hidden_slice
    )
    w_local = w_down[0].reshape(hidden_slice, n_section, d_slice)
    recv = lax.all_to_all(send, "expert", split_axis=0, concat_axis=0, tiled=True)
    recv = recv.reshape(slot_count, d_slice + hidden_slice)
    half = slot_count // 2
    first = recv[:half]
    second = recv[half:]
    gathered_first = lax.all_gather(first[:, :d_slice], "section", axis=0, tiled=False)
    spread = jnp.broadcast_to(second[None, :, :d_slice], (n_section, slot_count - half, d_slice))
    gathered_second = lax.all_to_all(spread, "section", split_axis=0, concat_axis=0, tiled=True)
    received = [(first[:, d_slice:], gathered_first), (second[:, d_slice:], gathered_second)]
    weight_acc = None
    returning = []
    for recv_scaled, gathered in received:
        unscaled = jnp.einsum("srd,hsd->rh", gathered, w_local, preferred_element_type=jnp.float32)
        returning.append(unscaled.astype(jnp.bfloat16))
        term = jnp.einsum("rh,srd->hsd", recv_scaled, gathered, preferred_element_type=jnp.float32)
        weight_acc = term if weight_acc is None else weight_acc + term
    weight_part = weight_acc.astype(jnp.bfloat16).reshape(1, hidden_slice, n_section * d_slice)
    grad_w = lax.psum_scatter(weight_part, "dp", scatter_dimension=2, tiled=True)
    returning = jnp.concatenate(returning, axis=0).reshape(experts, capacity, hidden_slice)
    returned = lax.all_to_all(returning, "expert", split_axis=0, concat_axis=0, tiled=True)
    unscaled_tok = lax.dot_general(
        sel_pairs,
        returned.reshape(slot_count, hidden_slice),
        (((0,), (0,)), ((), ())),
        preferred_element_type=jnp.float32,
    ).reshape(tok_count, top_count, hidden_slice)
    grad_hidden = (gate_weights[:, :, None] * unscaled_tok).astype(jnp.bfloat16)
    gate_share = jnp.sum(act.astype(jnp.float32) * unscaled_tok, axis=2)
    grad_gates = lax.psum(gate_share, "section")
    return (grad_hidden, grad_gates, grad_w)


def solution(mesh):
    placed = (
        P(("dp", "expert"), "section"),
        P(("dp", "expert"), None),
        P(("dp", "expert"), None),
        P(("dp", "expert"), None, "section"),
        P("expert", "section", None),
    )
    return jax.shard_map(
        local,
        mesh=mesh,
        in_specs=placed,
        out_specs=(
            P(("dp", "expert"), None, "section"),
            P(("dp", "expert"), None),
            P("expert", "section", "dp"),
        ),
        check_vma=False,
    )
```

profile of v0, /device:TPU:18, one launch (start us, length us, event | category | flops | bytes accessed | tf_op | source)
XLA Modules:
  0.0 324.6 jit_solution(13033326550447104199)
XLA Ops:
  7.2 0.0 copy-start
  7.2 0.0 all-gather.3.cloned.1.call-start
  7.2 0.8 fusion.33
  8.0 0.1 fusion.34
  8.1 0.7 select_reduce_fusion
  8.9 0.7 convert_add_fusion
  9.6 0.1 copy.29
  9.7 0.1 eq.67
  9.8 1.3 fusion.26
  11.1 2.5 fusion.8
  13.5 0.0 copy-done
  13.5 2.9 convolution_convert_fusion
  16.5 3.1 pad_maximum_fusion
  19.6 5.8 %copy.32 = bf16[1536,1152]{1,0:T(8,128)(2,1)} copy(bf16[1536,1152]{0,1:T(8,128)(2,1)} %pad_maximum_fusion) | data formatting | bytes 7077888 | tf_op jit(solution)/shard_map/concatenate | solution.py:45
  25.4 99.4 %all_to_all.15 = bf16[64,24,1152]{2,1,0:T(8,128)(2,1)S(1)} all-to-all(bf16[64,24,1152]{2,1,0:T(8,128)(2,1)} %bitcast.40), channel_id=1, replica_groups=mesh['dp'=2,'section'=4,'expert'=64] {'expert'}, dimensions={0} | all-to-all | bytes 7077888 | tf_op jit(solution)/shard_map/all_to_all | solution.py:49
  124.8 0.3 fusion.38
  125.0 0.0 copy-start.2
  125.1 0.0 copy-start.1
  125.1 1.3 copy-done.2
  126.3 1.2 slice.33
  127.5 0.0 all-gather.3.cloned.1.call-update
  127.5 0.1 slice.35
  127.7 2.8 broadcast_in_dim.16
  130.4 0.0 copy-done.1
  130.4 5.6 %all-to-all-start.1 = ((bf16[4,768,896]{2,1,0:T(8,128)(2,1)}), bf16[4,768,896]{2,1,0:T(8,128)(2,1)}, u32[]{:S(2)}, u32[]{:S(2)}) async-start(bf16[4,768,896]{2,1,0:T(8,128)(2,1)} %broadcast_in_dim.16), calls=%async_computation.1 | async-start | bytes 11010048 | tf_op jit(solution)/shard_map/all_to_all | solution.py:56
  136.1 0.0 reduce-scatter.2.cloned.1.call-start
  136.1 102.4 %all-gather.3.cloned.1.call-done = bf16[3072,896]{1,0:T(8,128)(2,1)} async-done(((bf16[768,896]{1,0:T(8,128)(2,1)}), bf16[3072,896]{1,0:T(8,128)(2,1)}) %all-gather.3.cloned.1.call-update) | async-done | bytes 5505040 | tf_op jit(solution)/shard_map/all_gather | solution.py:54
  238.4 6.1 %fusion.30 = f32[256,4,896]{2,0,1:T(8,128)} fusion(bf16[4,768,896]{2,1,0:T(8,128)(2,1)} %bitcast.46, bf16[768,1152]{1,0:T(8,128)(2,1)} %bitcast.45), kind=kOutput, calls=%fused_computation.33 | convolution fusion | flops 1409286144 | bytes 9568256 | tf_op jit(solution)/shard_map/rh,srd->hsd/dot_general | solution.py:63
  244.5 0.0 all-to-all-done.1
  244.6 5.4 %add_convert_fusion = bf16[256,4,896]{2,0,1:T(8,128)(2,1)S(1)} fusion(f32[256,4,896]{2,0,1:T(8,128)} %fusion.30, bf16[4,768,896]{2,1,0:T(8,128)(2,1)} %all-to-all-done.1, bf16[768,1152]{1,0:T(8,128)(2,1)} %bitcast.43), kind=kOutput, calls=%fused_computation.6 | convolution fusion | flops 1411121152 | bytes 11403264 | tf_op jit(solution)/shard_map/rh,srd->hsd/dot_general | solution.py:63
  250.0 2.4 copy.37
  252.4 0.0 reduce-scatter.2.cloned.1.call-update
  252.4 0.0 slice-start
  252.4 3.4 %reshape_squeeze.3 = bf16[256,4,896]{2,1,0:T(4,128)(2,1)S(1)} reshape(bf16[1,256,3584]{2,1,0:T(8,128)(2,1)} %param.9) | data formatting | bytes 3670016 | tf_op jit(solution)/shard_map/reshape;squeeze | solution.py:48
  255.9 0.0 slice-start.1
  255.9 4.3 %fusion.20 = bf16[768,256]{1,0:T(8,128)(2,1)S(1)} fusion(bf16[4,768,896]{2,1,0:T(8,128)(2,1)} %all-to-all-done.1, bf16[256,4,896]{2,1,0:T(4,128)(2,1)S(1)} %reshape_squeeze.3), kind=kOutput, calls=%fused_computation.22 | convolution fusion | flops 1409482752 | bytes 7733248 | tf_op jit(solution)/shard_map/srd,hsd->rh/dot_general | solution.py:61
  260.2 0.0 slice-done
  260.2 0.0 slice-done.1
  260.2 0.0 copy-start.3
  260.3 0.0 copy-start.4
  260.3 1.6 fusion.23
  261.9 0.1 pad_maximum_fusion.1
  262.0 38.3 %all_to_all.16 = bf16[64,24,256]{2,1,0:T(8,128)(2,1)S(1)} all-to-all(bf16[64,24,256]{2,1,0:T(8,128)(2,1)S(1)} %bitcast.50), channel_id=1, replica_groups=mesh['dp'=2,'section'=4,'expert'=64] {'expert'}, dimensions={0} | all-to-all | bytes 1572864 | tf_op jit(solution)/shard_map/all_to_all | solution.py:68
  300.2 0.0 copy-done.3
  300.2 0.0 copy-done.4
  300.2 1.4 fusion.27
  301.6 1.1 copy.38
  302.7 12.8 %psum.7 = f32[128,8]{0,1:T(8,128)} all-reduce(f32[128,8]{0,1:T(8,128)S(1)} %get-tuple-element.14), channel_id=1, replica_groups=mesh['dp'=2,'section'=4,'expert'=64] {'section'}, use_global_device_ids=true, to_apply=%region_3.4 | all-reduce | flops 1024 | bytes 8192 | tf_op jit(solution)/shard_map/psum | solution.py:77
  315.6 0.0 reduce-scatter.2.cloned.1.call-done
  315.6 2.2 copy.39
  (2 shorter events, 0.0 us)
Async XLA Ops:
  7.2 6.4 %copy-start = (bf16[128,896]{1,0:T(8,128)(2,1)S(1)}, bf16[128,896]{1,0:T(8,128)(2,1)}, u32[]{:S(2)}) copy-start(bf16[128,896]{1,0:T(8,128)(2,1)} %param.5) | copy-start | bytes 688132
  7.2 231.2 %all-gather.3.cloned.1.call-start = ((), (), s32[]{:S(2)}) async-start(), calls=%async_computation.5 | async-start | bytes 6881280 | tf_op jit(solution)/shard_map/all_gather | solution.py:54
  125.0 1.3 copy-start.2
  125.1 5.4 %copy-start.1 = (bf16[32,24,1152]{2,1,0:T(8,128)(2,1)}, bf16[32,24,1152]{2,1,0:T(8,128)(2,1)S(1)}, u32[]{:S(2)}) copy-start(bf16[32,24,1152]{2,1,0:T(8,128)(2,1)S(1)} %get-tuple-element.13) | copy-start | bytes 5308420
  130.4 114.1 %all-to-all-start.1 = ((bf16[4,768,896]{2,1,0:T(8,128)(2,1)}), bf16[4,768,896]{2,1,0:T(8,128)(2,1)}, u32[]{:S(2)}, u32[]{:S(2)}) async-start(bf16[4,768,896]{2,1,0:T(8,128)(2,1)} %broadcast_in_dim.16), calls=%async_computation.1 | async-start | bytes 11010048 | tf_op jit(solution)/shard_map/all_to_all | solution.py:56
  136.1 179.5 %reduce-scatter.2.cloned.1.call-start = ((), (), s32[]{:S(2)}) async-start(), calls=%async_computation.4 | async-start | bytes 2752512 | tf_op jit(solution)/shard_map/reduce_scatter | solution.py:66
  252.4 7.8 %slice-start = ((s8[5505024]{0:T(1024)(128)(4,1)}), s8[1310720]{0:T(1024)(128)(4,1)S(1)}, s32[]{:S(2)}) async-start(s8[5505024]{0:T(1024)(128)(4,1)} %bitcast.47), calls=%async_computation.6 | async-start | bytes 2621440
  255.9 4.4 %slice-start.1 = ((s8[5505024]{0:T(1024)(128)(4,1)}), s8[4194304]{0:T(1024)(128)(4,1)S(1)}, s32[]{:S(2)}) async-start(s8[5505024]{0:T(1024)(128)(4,1)} %bitcast.47), calls=%async_computation.7 | async-start | bytes 8388608
  260.2 40.0 %copy-start.3 = (bf16[128,8,256]{2,1,0:T(8,128)(2,1)S(1)}, bf16[128,8,256]{2,1,0:T(8,128)(2,1)}, u32[]{:S(2)}) copy-start(bf16[128,8,256]{2,1,0:T(8,128)(2,1)} %param.8) | copy-start | bytes 1572868
  260.3 40.0 %copy-start.4 = (f32[128,8]{0,1:T(8,128)S(1)}, f32[128,8]{0,1:T(8,128)}, u32[]{:S(2)}) copy-start(f32[128,8]{0,1:T(8,128)} %param.7) | copy-start | bytes 12292
Sparse Core Ops, SparseCore 0:
  127.7 110.7 all-gather.2
  252.6 22.7 reduce-scatter.1
where the time goes:
time: 325 us
  blocking collectives  151 us (46%)
  waiting for transfers between devices  102 us (31%)
  matrix products  24.5 us (8%)
  local copies, waits for them, and re-layouts  20.8 us (6%)
  between operations  14.2 us (4%)
  other arithmetic  6.64 us (2%)
  starting transfers between devices  5.67 us (2%)
    all_gather x1, waiting for transfers between devices, local(): lax.all_gather(first[:, :d_slice], 'section', axis=0, tiled=False)  102 us
    all_to_all x1, blocking collectives, local(): lax.all_to_all(send, 'expert', split_axis=0, concat_axis=0, tiled=True)  99.4 us
    all_to_all x1, blocking collectives, local(): lax.all_to_all(returning, 'expert', split_axis=0, concat_axis=0, tiled=True)  38.3 us
    psum x1, blocking collectives, local(): grad_gates = lax.psum(gate_share, 'section')  12.8 us
    dot_general x2, matrix products, local(): jnp.einsum('rh,srd->hsd', recv_scaled, gathered, preferred_element_type=j...  11.5 us
  transfers between devices with their start and end apart: 3, of which 1 were waited for; matrix products, arithmetic and copies ran while one was open for 6% of the time, Pallas kernels for 0%

commit v1 on v0

--- a/solution.py
+++ b/solution.py
@@ -74,7 +74,11 @@
     ).reshape(tok_count, top_count, hidden_slice)
     grad_hidden = (gate_weights[:, :, None] * unscaled_tok).astype(jnp.bfloat16)
     gate_share = jnp.sum(act.astype(jnp.float32) * unscaled_tok, axis=2)
-    grad_gates = lax.psum(gate_share, "section")
+    grad_gates = gate_share
+    for hop in (1, 2):
+        grad_gates = grad_gates + lax.ppermute(
+            grad_gates, "section", [(dev, dev ^ hop) for dev in range(4)]
+        )
     return (grad_hidden, grad_gates, grad_w)
 
 

time: 325 us -> 328 us (level)
  the two profiles are of different devices: /device:TPU:18 before, /device:TPU:20 now
where the time goes in v1:
time: 328 us; the launch traced here: 327 us
  blocking collectives  141 us (43%)
  waiting for transfers between devices  111 us (34%)
  matrix products  24.4 us (7%)
  local copies, waits for them, and re-layouts  20.7 us (6%)
  between operations  14.2 us (4%)
  starting transfers between devices  9.45 us (3%)
  other arithmetic  7.23 us (2%)
    all_gather x1, waiting for transfers between devices, local(): lax.all_gather(first[:, :d_slice], 'section', axis=0, tiled=False)  103 us
    all_to_all x1, blocking collectives, local(): lax.all_to_all(send, 'expert', split_axis=0, concat_axis=0, tiled=True)  99.4 us
    all_to_all x1, blocking collectives, local(): lax.all_to_all(returning, 'expert', split_axis=0, concat_axis=0, tiled=True)  41.2 us
    dot_general x2, matrix products, local(): jnp.einsum('rh,srd->hsd', recv_scaled, gathered, preferred_element_type=j...  11.5 us
    ppermute x2, waiting for transfers between devices, local(): lax.ppermute(grad_gates, 'section', [(dev, dev ^ hop) for dev in range(4)])  7.56 us
  transfers between devices with their start and end apart: 5, of which 3 were waited for; matrix products, arithmetic and copies ran while one was open for 7% of the time, Pallas kernels for 0%

profile of v1, /device:TPU:20, one launch (start us, length us, event | category | flops | bytes accessed | tf_op | source)
XLA Modules:
  0.0 327.4 jit_solution(318271343807478779)
XLA Ops:
  7.2 0.0 copy-start
  7.2 0.0 all-gather.3.cloned.1.call-start
  7.2 0.8 fusion.33
  8.0 0.1 fusion.34
  8.1 0.7 select_reduce_fusion
  8.9 0.7 convert_add_fusion
  9.6 0.1 copy.29
  9.7 0.1 eq.67
  9.8 1.3 fusion.26
  11.1 2.5 fusion.8
  13.5 0.0 copy-done
  13.5 2.9 convolution_convert_fusion
  16.5 3.1 pad_maximum_fusion
  19.6 5.8 %copy.32 = bf16[1536,1152]{1,0:T(8,128)(2,1)} copy(bf16[1536,1152]{0,1:T(8,128)(2,1)} %pad_maximum_fusion) | data formatting | bytes 7077888 | tf_op jit(solution)/shard_map/concatenate | solution.py:45
  25.4 99.4 %all_to_all.15 = bf16[64,24,1152]{2,1,0:T(8,128)(2,1)S(1)} all-to-all(bf16[64,24,1152]{2,1,0:T(8,128)(2,1)} %bitcast.40), channel_id=1, replica_groups=mesh['dp'=2,'section'=4,'expert'=64] {'expert'}, dimensions={0} | all-to-all | bytes 7077888 | tf_op jit(solution)/shard_map/all_to_all | solution.py:49
  124.8 0.3 fusion.38
  125.1 0.0 copy-start.2
  125.1 0.0 copy-start.1
  125.1 1.2 copy-done.2
  126.3 1.2 slice.33
  127.5 0.0 all-gather.3.cloned.1.call-update
  127.5 0.1 slice.35
  127.6 2.8 broadcast_in_dim.16
  130.4 0.0 copy-done.1
  130.4 5.6 %all-to-all-start.1 = ((bf16[4,768,896]{2,1,0:T(8,128)(2,1)}), bf16[4,768,896]{2,1,0:T(8,128)(2,1)}, u32[]{:S(2)}, u32[]{:S(2)}) async-start(bf16[4,768,896]{2,1,0:T(8,128)(2,1)} %broadcast_in_dim.16), calls=%async_computation.1 | async-start | bytes 11010048 | tf_op jit(solution)/shard_map/all_to_all | solution.py:56
  136.0 0.0 reduce-scatter.2.cloned.1.call-start
  136.0 103.2 %all-gather.3.cloned.1.call-done = bf16[3072,896]{1,0:T(8,128)(2,1)} async-done(((bf16[768,896]{1,0:T(8,128)(2,1)}), bf16[3072,896]{1,0:T(8,128)(2,1)}) %all-gather.3.cloned.1.call-update) | async-done | bytes 5505040 | tf_op jit(solution)/shard_map/all_gather | solution.py:54
  239.1 6.1 %fusion.30 = f32[256,4,896]{2,0,1:T(8,128)} fusion(bf16[4,768,896]{2,1,0:T(8,128)(2,1)} %bitcast.46, bf16[768,1152]{1,0:T(8,128)(2,1)} %bitcast.45), kind=kOutput, calls=%fused_computation.33 | convolution fusion | flops 1409286144 | bytes 9568256 | tf_op jit(solution)/shard_map/rh,srd->hsd/dot_general | solution.py:63
  245.2 0.0 all-to-all-done.1
  245.2 5.4 %add_convert_fusion = bf16[256,4,896]{2,0,1:T(8,128)(2,1)S(1)} fusion(f32[256,4,896]{2,0,1:T(8,128)} %fusion.30, bf16[4,768,896]{2,1,0:T(8,128)(2,1)} %all-to-all-done.1, bf16[768,1152]{1,0:T(8,128)(2,1)} %bitcast.43), kind=kOutput, calls=%fused_computation.6 | convolution fusion | flops 1411121152 | bytes 11403264 | tf_op jit(solution)/shard_map/rh,srd->hsd/dot_general | solution.py:63
  250.7 2.4 copy.37
  253.1 0.0 reduce-scatter.2.cloned.1.call-update
  253.1 0.0 slice-start
  253.1 3.4 %reshape_squeeze.3 = bf16[256,4,896]{2,1,0:T(4,128)(2,1)S(1)} reshape(bf16[1,256,3584]{2,1,0:T(8,128)(2,1)} %param.9) | data formatting | bytes 3670016 | tf_op jit(solution)/shard_map/reshape;squeeze | solution.py:48
  256.5 0.0 slice-start.1
  256.6 4.3 %fusion.20 = bf16[768,256]{1,0:T(8,128)(2,1)S(1)} fusion(bf16[4,768,896]{2,1,0:T(8,128)(2,1)} %all-to-all-done.1, bf16[256,4,896]{2,1,0:T(4,128)(2,1)S(1)} %reshape_squeeze.3), kind=kOutput, calls=%fused_computation.22 | convolution fusion | flops 1409482752 | bytes 7733248 | tf_op jit(solution)/shard_map/srd,hsd->rh/dot_general | solution.py:61
  260.9 0.0 slice-done
  260.9 0.0 slice-done.1
  260.9 0.0 copy-start.3
  260.9 0.0 copy-start.4
  260.9 1.6 fusion.23
  262.6 0.1 pad_maximum_fusion.1
  262.6 41.2 %all_to_all.16 = bf16[64,24,256]{2,1,0:T(8,128)(2,1)S(1)} all-to-all(bf16[64,24,256]{2,1,0:T(8,128)(2,1)S(1)} %bitcast.50), channel_id=1, replica_groups=mesh['dp'=2,'section'=4,'expert'=64] {'expert'}, dimensions={0} | all-to-all | bytes 1572864 | tf_op jit(solution)/shard_map/all_to_all | solution.py:68
  303.8 0.0 copy-done.3
  303.8 0.0 copy-done.4
  303.8 1.4 fusion.27
  305.2 1.9 collective-permute-start
  307.1 3.6 %collective-permute-done = f32[128,8]{0,1:T(8,128)S(1)} collective-permute-done((f32[128,8]{0,1:T(8,128)S(1)}, f32[128,8]{0,1:T(8,128)S(1)}, u32[]{:S(2)}, u32[]{:S(2)}) %collective-permute-start) | collective-permute-done | bytes 4128 | tf_op jit(solution)/shard_map/ppermute | solution.py:79
  310.7 1.9 collective-permute-start.1
  312.6 1.1 copy.38
  313.7 4.0 %collective-permute-done.1 = f32[128,8]{0,1:T(8,128)S(1)} collective-permute-done((f32[128,8]{0,1:T(8,128)S(1)}, f32[128,8]{0,1:T(8,128)S(1)}, u32[]{:S(2)}, u32[]{:S(2)}) %collective-permute-start.1) | collective-permute-done | bytes 4128 | tf_op jit(solution)/shard_map/ppermute | solution.py:79
  317.7 0.6 add.22
  318.3 0.0 reduce-scatter.2.cloned.1.call-done
  318.3 2.2 copy.39
  (3 shorter events, 0.0 us)
Async XLA Ops:
  7.2 6.4 %copy-start = (bf16[128,896]{1,0:T(8,128)(2,1)S(1)}, bf16[128,896]{1,0:T(8,128)(2,1)}, u32[]{:S(2)}) copy-start(bf16[128,896]{1,0:T(8,128)(2,1)} %param.5) | copy-start | bytes 688132
  7.2 232.0 %all-gather.3.cloned.1.call-start = ((), (), s32[]{:S(2)}) async-start(), calls=%async_computation.5 | async-start | bytes 6881280 | tf_op jit(solution)/shard_map/all_gather | solution.py:54
  125.1 1.2 copy-start.2
  125.1 5.3 %copy-start.1 = (bf16[32,24,1152]{2,1,0:T(8,128)(2,1)}, bf16[32,24,1152]{2,1,0:T(8,128)(2,1)S(1)}, u32[]{:S(2)}) copy-start(bf16[32,24,1152]{2,1,0:T(8,128)(2,1)S(1)} %get-tuple-element.13) | copy-start | bytes 5308420
  130.4 114.8 %all-to-all-start.1 = ((bf16[4,768,896]{2,1,0:T(8,128)(2,1)}), bf16[4,768,896]{2,1,0:T(8,128)(2,1)}, u32[]{:S(2)}, u32[]{:S(2)}) async-start(bf16[4,768,896]{2,1,0:T(8,128)(2,1)} %broadcast_in_dim.16), calls=%async_computation.1 | async-start | bytes 11010048 | tf_op jit(solution)/shard_map/all_to_all | solution.py:56
  136.0 182.3 %reduce-scatter.2.cloned.1.call-start = ((), (), s32[]{:S(2)}) async-start(), calls=%async_computation.4 | async-start | bytes 2752512 | tf_op jit(solution)/shard_map/reduce_scatter | solution.py:66
  253.1 7.8 %slice-start = ((s8[5505024]{0:T(1024)(128)(4,1)}), s8[1310720]{0:T(1024)(128)(4,1)S(1)}, s32[]{:S(2)}) async-start(s8[5505024]{0:T(1024)(128)(4,1)} %bitcast.47), calls=%async_computation.6 | async-start | bytes 2621440
  256.5 4.4 %slice-start.1 = ((s8[5505024]{0:T(1024)(128)(4,1)}), s8[4194304]{0:T(1024)(128)(4,1)S(1)}, s32[]{:S(2)}) async-start(s8[5505024]{0:T(1024)(128)(4,1)} %bitcast.47), calls=%async_computation.7 | async-start | bytes 8388608
  260.9 42.9 %copy-start.3 = (bf16[128,8,256]{2,1,0:T(8,128)(2,1)S(1)}, bf16[128,8,256]{2,1,0:T(8,128)(2,1)}, u32[]{:S(2)}) copy-start(bf16[128,8,256]{2,1,0:T(8,128)(2,1)} %param.8) | copy-start | bytes 1572868
  260.9 42.9 %copy-start.4 = (f32[128,8]{0,1:T(8,128)S(1)}, f32[128,8]{0,1:T(8,128)}, u32[]{:S(2)}) copy-start(f32[128,8]{0,1:T(8,128)} %param.7) | copy-start | bytes 12292
  305.2 5.5 %collective-permute-start = (f32[128,8]{0,1:T(8,128)S(1)}, f32[128,8]{0,1:T(8,128)S(1)}, u32[]{:S(2)}, u32[]{:S(2)}) collective-permute-start(f32[128,8]{0,1:T(8,128)S(1)} %get-tuple-element.14), channel_id=1, source_target_pairs={{0,64},{64,0},{128,192},{192,128},{1,65},{65,1},{129,193},{193,129... | collective-permute-start | bytes 12296 | tf_op jit(solution)/shard_map/ppermute | solution.py:79
  310.7 7.0 %collective-permute-start.1 = (f32[128,8]{0,1:T(8,128)S(1)}, f32[128,8]{0,1:T(8,128)S(1)}, u32[]{:S(2)}, u32[]{:S(2)}) collective-permute-start(f32[128,8]{0,1:T(8,128)S(1)} %add.21), channel_id=1, source_target_pairs={{0,128},{64,192},{128,0},{192,64},{1,129},{65,193},{129,1},{193,65... | collective-permute-start | bytes 12296 | tf_op jit(solution)/shard_map/ppermute | solution.py:79
Sparse Core Ops, SparseCore 0:
  127.6 111.4 all-gather.2
  253.2 21.9 reduce-scatter.1
